TPU v7x, 128 devices: a whole 4x4x4 slice. The times are simulated.
128 devices in a mesh: row: 8 (over z_hi, x), col: 16 (over z_lo, y, core).
Axes of the slice: x: 4, y: 4, z: 4 (z_hi: 2, z_lo: 2; z = z_hi * 2 + z_lo), core: 2. Of those that a mesh axis runs over, the one named last changes fastest.
Arguments:
- tokens: bfloat16 [1024, 8192], P(('row', 'col')), may hold values from -6 to 6
- gain: float32 [8192], replicated, may hold values from 0.5 to 1.5
- grad_out: bfloat16 [1024, 8192], P(('row', 'col')), may hold values from -4 to 4
- pre_gate: bfloat16 [1024, 28672], P('col', 'row'), may hold values from -6 to 6
- pre_up: bfloat16 [1024, 28672], P('col', 'row'), may hold values from -6 to 6
- gate_weight: bfloat16 [8192, 28672], P('col', 'row'), may hold values from -0.0625 to 0.0625
- up_weight: bfloat16 [8192, 28672], P('col', 'row'), may hold values from -0.0625 to 0.0625
- down_weight: bfloat16 [28672, 8192], P('row', 'col'), may hold values from -0.03125 to 0.03125
Outputs:
- grad_tokens: bfloat16 [1024, 8192], P(('row', 'col'))
- grad_gain: float32 [8192], replicated
- grad_gate: bfloat16 [8192, 28672], P('col', 'row')
- grad_up: bfloat16 [8192, 28672], P('col', 'row')
- grad_down: bfloat16 [28672, 8192], P('row', 'col')
All inputs are finite; a program needn't handle non-finite values.
Results may differ from a plain program's by a relative error of at most 0.0057.
Values may be sent and summed in bfloat16 or wider, within the bound.
No kernel may reach another device: no remote copies, remote signals or barrier semaphores. Data moves between devices by JAX's collectives and lax.ppermute only.
A program may use at most 192 MiB of HBM per device.

v0:
```python
import jax
import jax.numpy as jnp
from jax import lax
from jax.sharding import PartitionSpec as P

epsilon = 1e-05


def swiglu_grads(hidden_grad, pre_gate, pre_up):
    gate_wide = pre_gate.astype(jnp.float32)
    up_wide = pre_up.astype(jnp.float32)
    sigmoid = jax.nn.sigmoid(gate_wide)
    silu = gate_wide * sigmoid
    hidden = (silu * up_wide).astype(jnp.bfloat16)
    up_grad = (hidden_grad * silu).astype(jnp.bfloat16)
    gate_grad = (hidden_grad * up_wide * sigmoid * (1.0 + gate_wide * (1.0 - sigmoid))).astype(
        jnp.bfloat16
    )
    return (hidden, gate_grad, up_grad)


def local(tokens, gain, grad_out, pre_gate, pre_up, gate_weight, up_weight, down_weight):
    tokens_wide = tokens.astype(jnp.float32)
    inverse_rms = lax.rsqrt(jnp.mean(tokens_wide * tokens_wide, axis=1, keepdims=True) + epsilon)
    normed = tokens_wide * inverse_rms
    scaled = (normed * gain).astype(jnp.bfloat16)
    grid_input, grid_grad = (
        lax.all_to_all(scaled, "col", split_axis=1, concat_axis=0, tiled=True),
        lax.all_to_all(grad_out, "col", split_axis=1, concat_axis=0, tiled=True),
    )
    all_input, all_grad = (
        lax.all_gather(grid_input, "row", axis=0, tiled=True),
        lax.all_gather(grid_grad, "row", axis=0, tiled=True),
    )
    partial_grad = jnp.einsum(
        "td,fd->tf", all_grad, down_weight, preferred_element_type=jnp.float32
    )
    block_grad = lax.psum_scatter(partial_grad, "col", scatter_dimension=0, tiled=True)
    hidden_block, gate_block, up_block = swiglu_grads(block_grad, pre_gate, pre_up)
    gate_piece = lax.all_gather(gate_block, "col", axis=0, tiled=True)
    up_piece = lax.all_gather(up_block, "col", axis=0, tiled=True)
    hidden_piece = lax.all_gather(hidden_block, "col", axis=0, tiled=True)
    new_rows = jnp.einsum("tf,df->td", gate_piece, gate_weight, preferred_element_type=jnp.float32)
    new_rows = new_rows + jnp.einsum(
        "tf,df->td", up_piece, up_weight, preferred_element_type=jnp.float32
    )
    gate_total = jnp.einsum("td,tf->df", all_input, gate_piece, preferred_element_type=jnp.float32)
    up_total = jnp.einsum("td,tf->df", all_input, up_piece, preferred_element_type=jnp.float32)
    down_total = jnp.einsum("tf,td->fd", hidden_piece, all_grad, preferred_element_type=jnp.float32)
    grid_back = lax.psum_scatter(new_rows, "row", scatter_dimension=0, tiled=True)
    normed_grad = lax.all_to_all(grid_back, "col", split_axis=0, concat_axis=1, tiled=True)
    gain_terms = jnp.sum(normed_grad * normed, axis=0)
    grad_gain = lax.psum(lax.psum(gain_terms, "col"), "row")
    scaled_grad = normed_grad * gain
    inner = jnp.mean(scaled_grad * normed, axis=1, keepdims=True)
    grad_tokens = (
        grad_out.astype(jnp.float32) + inverse_rms * (scaled_grad - normed * inner)
    ).astype(jnp.bfloat16)
    return (
        grad_tokens,
        grad_gain,
        gate_total.astype(jnp.bfloat16),
        up_total.astype(jnp.bfloat16),
        down_total.astype(jnp.bfloat16),
    )


def solution(mesh):
    in_specs = (
        P(("row", "col"), None),
        P(),
        P(("row", "col"), None),
        P("col", "row"),
        P("col", "row"),
        P("col", "row"),
        P("col", "row"),
        P("row", "col"),
    )
    out_specs = (P(("row", "col"), None), P(), P("col", "row"), P("col", "row"), P("row", "col"))
    return jax.shard_map(local, mesh=mesh, in_specs=in_specs, out_specs=out_specs, check_vma=False)
```

profile of v0, /device:TPU:0, one launch (start us, length us, event | category | flops | bytes accessed | tf_op | source)
XLA Modules:
  0.0 544.2 jit_solution(9490995752814410187)
XLA Ops:
  7.2 0.0 all-gather.6.cloned.1.call-start
  7.2 12.6 %all_to_all.57 = bf16[8,16,512]{2,0,1:T(8,128)(2,1)} all-to-all(bf16[8,16,512]{2,0,1:T(8,128)(2,1)} %bitcast.28), channel_id=1, replica_groups=mesh['row'=8,'col'=16] {'col'}, dimensions={1} | all-to-all | bytes 262144 | tf_op jit(solution)/shard_map/all_to_all | solution.py:29
  19.9 0.0 all-gather.6.cloned.1.call-update
  19.9 0.0 reduce-scatter.3.cloned.1.call-start
  19.9 47.1 %all-gather.6.cloned.1.call-done = bf16[1024,512]{1,0:T(8,128)(2,1)} async-done(((bf16[128,512]{1,0:T(8,128)(2,1)}), bf16[1024,512]{1,0:T(8,128)(2,1)}) %all-gather.6.cloned.1.call-update) | async-done | bytes 1048592 | tf_op jit(solution)/shard_map/all_gather | solution.py:33
  67.1 11.6 %fusion.20 = f32[1024,3584]{1,0:T(8,128)} fusion(bf16[1024,512]{1,0:T(8,128)(2,1)} %all-gather.6.cloned.1.call-done, bf16[3584,512]{1,0:T(8,128)(2,1)} %param.15), kind=kOutput, calls=%fused_computation.34 | convolution fusion | flops 3758096384 | bytes 19398656 | tf_op jit(solution)/shard_map/td,fd->tf/dot_general | solution.py:35
  78.6 0.0 reduce-scatter.3.cloned.1.call-update
  78.7 0.0 all-gather.8.cloned.1.call-start
  78.7 88.0 %reduce-scatter.3.cloned.1.call-done = f32[64,3584]{1,0:T(8,128)} async-done(((f32[1024,3584]{1,0:T(8,128)}), f32[64,3584]{1,0:T(8,128)}) %reduce-scatter.3.cloned.1.call-update) | async-done | bytes 917520 | tf_op jit(solution)/shard_map/reduce_scatter | solution.py:38
  166.7 0.0 copy-done.3
  166.7 0.0 copy-done.4
  166.7 2.7 multiply_convert_fusion
  169.3 0.0 all-gather.8.cloned.1.call-update
  169.4 0.0 all-gather.10.cloned.1.call-start
  169.4 0.5 all-gather.10.cloned.1.call-update
  169.9 0.0 reduce-scatter.5.cloned.1.call-start
  170.0 46.0 %all-gather.8.cloned.1.call-done = bf16[1024,3584]{1,0:T(8,128)(2,1)} async-done(((bf16[64,3584]{1,0:T(8,128)(2,1)}), bf16[1024,3584]{1,0:T(8,128)(2,1)}) %all-gather.8.cloned.1.call-update) | async-done | bytes 7340048 | tf_op jit(solution)/shard_map/all_gather | solution.py:40
  216.0 9.4 %fusion.21 = f32[1024,512]{1,0:T(8,128)} fusion(bf16[1024,3584]{1,0:T(8,128)(2,1)} %all-gather.8.cloned.1.call-done, bf16[512,3584]{1,0:T(8,128)(2,1)} %param.13), kind=kOutput, calls=%fused_computation.35 | convolution fusion | flops 3758096384 | bytes 13107200 | tf_op jit(solution)/shard_map/tf,df->td/dot_general | solution.py:43
  225.5 40.7 %all-gather.10.cloned.1.call-done = bf16[1024,3584]{1,0:T(8,128)(2,1)} async-done(((bf16[64,3584]{1,0:T(8,128)(2,1)}), bf16[1024,3584]{1,0:T(8,128)(2,1)}) %all-gather.10.cloned.1.call-update) | async-done | bytes 7340048 | tf_op jit(solution)/shard_map/all_gather | solution.py:41
  266.2 10.1 %convolution_add_fusion = f32[1024,512]{1,0:T(8,128)} fusion(f32[1024,512]{1,0:T(8,128)} %fusion.21, bf16[1024,3584]{1,0:T(8,128)(2,1)} %all-gather.10.cloned.1.call-done, bf16[512,3584]{1,0:T(8,128)(2,1)} %param.14), kind=kOutput, calls=%fused_computation.3 | convolution fusion | flops 3758620672 | bytes 15204352 | tf_op jit(solution)/shard_map/tf,df->td/dot_general | solution.py:44
  276.3 0.0 reduce-scatter.5.cloned.1.call-update
  276.3 0.0 all-gather.14.cloned.1.call-start
  276.4 0.5 all-gather.14.cloned.1.call-update
  276.9 0.0 copy-done
  276.9 0.2 fusion.19
  277.1 76.9 %reduce-scatter.5.cloned.1.call-done = f32[128,512]{1,0:T(8,128)} async-done(((f32[1024,512]{1,0:T(8,128)}), f32[128,512]{1,0:T(8,128)}) %reduce-scatter.5.cloned.1.call-update) | async-done | bytes 262160 | tf_op jit(solution)/shard_map/reduce_scatter | solution.py:50
  354.0 4.5 all-to-all-start.1
  358.4 0.0 copy-start.5
  358.4 0.0 copy-start.2
  358.5 43.7 %all-gather.14.cloned.1.call-done = bf16[1024,3584]{1,0:T(8,128)(2,1)} async-done(((bf16[64,3584]{1,0:T(8,128)(2,1)}), bf16[1024,3584]{1,0:T(8,128)(2,1)}) %all-gather.14.cloned.1.call-update) | async-done | bytes 7340048 | tf_op jit(solution)/shard_map/all_gather | solution.py:42
  402.2 0.0 copy-done.6
  402.2 8.6 %convolution_convert_fusion = bf16[3584,512]{1,0:T(8,128)(2,1)} fusion(bf16[1024,3584]{1,0:T(8,128)(2,1)} %all-gather.14.cloned.1.call-done, bf16[1024,512]{1,0:T(8,128)(2,1)S(1)} %copy-done.6), kind=kOutput, calls=%fused_computation | convolution fusion | flops 3759931392 | bytes 12058624 | tf_op jit(solution)/shard_map/tf,td->fd/dot_general | solution.py:49
  410.8 0.0 all-to-all-done.1
  410.8 0.0 copy-done.5
  410.8 0.9 fusion.17
  411.7 4.7 all-to-all-start.2
  416.4 0.0 all-gather.12.cloned.1.call-start
  416.5 56.5 %psum.14 = f32[8192]{0:T(1024)S(1)} all-reduce(f32[8192]{0:T(1024)S(1)} %get-tuple-element.5), channel_id=1, replica_groups=mesh['row'=8,'col'=16] {'col'}, use_global_device_ids=true, to_apply=%region_5.0 | all-reduce | flops 8192 | bytes 65536 | tf_op jit(solution)/shard_map/psum | solution.py:53
  473.0 0.0 all-to-all-done.2
  473.0 0.7 copy-done.1
  473.6 0.0 all-gather.12.cloned.1.call-update
  473.7 42.3 %psum.15 = f32[8192]{0:T(1024)} all-reduce(f32[8192]{0:T(1024)S(1)} %psum.14), channel_id=1, replica_groups=mesh['row'=8,'col'=16] {'row'}, use_global_device_ids=true, to_apply=%region_6.0 | all-reduce | flops 8192 | bytes 65536 | tf_op jit(solution)/shard_map/psum | solution.py:53
  516.0 0.0 copy-done.2
  516.0 0.8 fusion.16
  516.8 2.7 all-gather.12.cloned.1.call-done
  519.5 9.3 %convolution_convert_fusion.2 = bf16[512,3584]{1,0:T(8,128)(2,1)} fusion(bf16[1024,512]{1,0:T(8,128)(2,1)} %all-gather.12.cloned.1.call-done, bf16[1024,3584]{1,0:T(8,128)(2,1)} %all-gather.8.cloned.1.call-done), kind=kOutput, calls=%fused_computation.2 | convolution fusion | flops 3759931392 | bytes 12058624 | tf_op jit(solution)/shard_map/td,tf->df/dot_general | solution.py:47
  528.8 0.0 copy-done.7
  528.8 8.5 %convolution_convert_fusion.1 = bf16[512,3584]{1,0:T(8,128)(2,1)} fusion(bf16[1024,512]{1,0:T(8,128)(2,1)S(1)} %copy-done.7, bf16[1024,3584]{1,0:T(8,128)(2,1)} %all-gather.10.cloned.1.call-done), kind=kOutput, calls=%fused_computation.1 | convolution fusion | flops 3759931392 | bytes 12058624 | tf_op jit(solution)/shard_map/td,tf->df/dot_general | solution.py:48
  (8 shorter events, 0.0 us)
Async XLA Ops:
  7.2 59.9 %all-gather.6.cloned.1.call-start = ((), (), s32[]{:S(2)}) async-start(), calls=%async_computation.5 | async-start | bytes 1179648 | tf_op jit(solution)/shard_map/all_gather | solution.py:33
  19.9 146.8 %reduce-scatter.3.cloned.1.call-start = ((), (), s32[]{:S(2)}) async-start(), calls=%async_computation.6 | async-start | bytes 15597568 | tf_op jit(solution)/shard_map/reduce_scatter | solution.py:38
  78.6 88.0 %copy-start.3 = (bf16[64,3584]{1,0:T(8,128)(2,1)S(1)}, bf16[64,3584]{1,0:T(8,128)(2,1)}, u32[]{:S(2)}) copy-start(bf16[64,3584]{1,0:T(8,128)(2,1)} %param.11) | copy-start | bytes 1376260
  78.6 88.0 %copy-start.4 = (bf16[64,3584]{1,0:T(8,128)(2,1)S(1)}, bf16[64,3584]{1,0:T(8,128)(2,1)}, u32[]{:S(2)}) copy-start(bf16[64,3584]{1,0:T(8,128)(2,1)} %param.12) | copy-start | bytes 1376260
  78.7 137.4 %all-gather.8.cloned.1.call-start = ((), (), s32[]{:S(2)}) async-start(), calls=%async_computation.7 | async-start | bytes 7798784 | tf_op jit(solution)/shard_map/all_gather | solution.py:40
  169.4 96.8 %all-gather.10.cloned.1.call-start = ((), (), s32[]{:S(2)}) async-start(), calls=%async_computation.8 | async-start | bytes 7798784 | tf_op jit(solution)/shard_map/all_gather | solution.py:41
  169.9 184.0 %reduce-scatter.5.cloned.1.call-start = ((), (), s32[]{:S(2)}) async-start(), calls=%async_computation.9 | async-start | bytes 2359296 | tf_op jit(solution)/shard_map/reduce_scatter | solution.py:50
  225.4 51.4 %copy-start = (bf16[8,8192]{1,0:T(8,128)(2,1)S(1)}, bf16[8,8192]{1,0:T(8,128)(2,1)}, u32[]{:S(2)}) copy-start(bf16[8,8192]{1,0:T(8,128)(2,1)} %param.8) | copy-start | bytes 393220
  225.4 176.8 %copy-start.6 = (bf16[1024,512]{1,0:T(8,128)(2,1)S(1)}, bf16[1024,512]{1,0:T(8,128)(2,1)}, u32[]{:S(2)}) copy-start(bf16[1024,512]{1,0:T(8,128)(2,1)} %all-gather.6.cloned.1.call-done) | copy-start | bytes 3145732
  276.3 125.9 %all-gather.14.cloned.1.call-start = ((), (), s32[]{:S(2)}) async-start(), calls=%async_computation.11 | async-start | bytes 7798784 | tf_op jit(solution)/shard_map/all_gather | solution.py:42
  354.0 56.8 %all-to-all-start.1 = ((f32[16,8,512]{2,1,0:T(8,128)}), f32[16,8,512]{2,1,0:T(8,128)S(1)}, u32[]{:S(2)}, u32[]{:S(2)}) async-start(f32[16,8,512]{2,1,0:T(8,128)} %bitcast.29), calls=%async_computation.3 | async-start | bytes 524288 | tf_op jit(solution)/shard_map/all_to_all | solution.py:51
  358.4 52.4 %copy-start.5 = (f32[8192]{0:T(1024)S(1)}, f32[8192]{0:T(1024)}, u32[]{:S(2)}) copy-start(f32[8192]{0:T(1024)} %param.9) | copy-start | bytes 98308
  358.4 157.6 %copy-start.2 = (bf16[8,8192]{1,0:T(8,128)(2,1)S(1)}, bf16[8,8192]{1,0:T(8,128)(2,1)}, u32[]{:S(2)}) copy-start(bf16[8,8192]{1,0:T(8,128)(2,1)} %param.10) | copy-start | bytes 393220
  411.7 61.3 %all-to-all-start.2 = ((bf16[8,16,512]{2,0,1:T(8,128)(2,1)}), bf16[8,16,512]{2,0,1:T(8,128)(2,1)S(1)}, u32[]{:S(2)}, u32[]{:S(2)}) async-start(bf16[8,16,512]{2,0,1:T(8,128)(2,1)} %bitcast.7), calls=%async_computation.4 | async-start | bytes 262144 | tf_op jit(solution)/shard_map/all_to_all | solution.py:28
  416.4 103.1 %all-gather.12.cloned.1.call-start = ((), (), s32[]{:S(2)}) async-start(), calls=%async_computation.10 | async-start | bytes 1179648 | tf_op jit(solution)/shard_map/all_gather | solution.py:32
  473.0 0.7 copy-start.1
  519.5 9.3 %copy-start.7 = (bf16[1024,512]{1,0:T(8,128)(2,1)S(1)}, bf16[1024,512]{1,0:T(8,128)(2,1)}, u32[]{:S(2)}) copy-start(bf16[1024,512]{1,0:T(8,128)(2,1)} %all-gather.12.cloned.1.call-done) | copy-start | bytes 3145732
Sparse Core Ops, SparseCore 0:
  20.0 47.0 all-gather.5
  78.8 87.8 reduce-scatter.2
  169.5 46.5 all-gather.7
  218.2 47.9 all-gather.9
  276.4 77.4 reduce-scatter.4
  356.1 46.0 all-gather.13
  473.8 45.6 all-gather.11
where the time goes:
time: 545 us; the launch traced here: 544 us
  waiting for transfers between devices  346 us (63%)
  blocking collectives  111 us (20%)
  matrix products  57.5 us (11%)
  between operations  14.2 us (3%)
  starting transfers between devices  9.43 us (2%)
    psum x2, blocking collectives, local(): grad_gain = lax.psum(lax.psum(gain_terms, 'col'), 'row')  98.9 us
    reduce_scatter x1, waiting for transfers between devices, local(): lax.psum_scatter(partial_grad, 'col', scatter_dimension=0, tiled=True)  88 us
    reduce_scatter x1, waiting for transfers between devices, local(): lax.psum_scatter(new_rows, 'row', scatter_dimension=0, tiled=True)  76.9 us
    all_gather x1, waiting for transfers between devices, local(): lax.all_gather(grid_grad, 'row', axis=0, tiled=True)  47.1 us
    all_gather x1, waiting for transfers between devices, local(): gate_piece = lax.all_gather(gate_block, 'col', axis=0, tiled=True)  46 us
    all_gather x1, waiting for transfers between devices, local(): hidden_piece = lax.all_gather(hidden_block, 'col', axis=0, tiled=True)  43.7 us
    all_gather x1, waiting for transfers between devices, local(): up_piece = lax.all_gather(up_block, 'col', axis=0, tiled=True)  40.7 us
    all_to_all x1, blocking collectives, local(): lax.all_to_all(grad_out, 'col', split_axis=1, concat_axis=0, tiled=True)  12.6 us
  transfers between devices with their start and end apart: 9, of which 7 were waited for; matrix products, arithmetic and copies ran while one was open for 3% of the time, Pallas kernels for 0%

commit v1 on v0

--- a/solution.py
+++ b/solution.py
@@ -50,7 +50,7 @@
     grid_back = lax.psum_scatter(new_rows, "row", scatter_dimension=0, tiled=True)
     normed_grad = lax.all_to_all(grid_back, "col", split_axis=0, concat_axis=1, tiled=True)
     gain_terms = jnp.sum(normed_grad * normed, axis=0)
-    grad_gain = lax.psum(lax.psum(gain_terms, "col"), "row")
+    grad_gain = lax.psum(jnp.sum(lax.all_gather(gain_terms, "col"), axis=0), "row")
     scaled_grad = normed_grad * gain
     inner = jnp.mean(scaled_grad * normed, axis=1, keepdims=True)
     grad_tokens = (

time: 545 us -> 514 us (0.943)
  blocking collectives: 111 us -> 74.8 us
  waiting for transfers between devices: 346 us -> 353 us
    psum x2 -> x1, blocking collectives: 98.9 us -> 42.2 us  [local(): lax.psum(jnp.sum(lax.all_gather(gain_terms, 'col'), axis=0), 'row')]
    all_gather x0 -> x1, blocking collectives: none -> 19.9 us  [local(): lax.all_gather(gain_terms, 'col')]
    all_to_all x1, waiting for transfers between devices: 0.01 us -> 6.3 us  [local(): lax.all_to_all(scaled, 'col', split_axis=1, concat_axis=0, tiled=True)]
  transfers between devices with their start and end apart: 9 -> 9, of which waited for: 7 -> 8; matrix products, arithmetic and copies ran while one was open for 3% -> 4% of each run, Pallas kernels for 0% -> 0%
where the time goes in v1:
time: 514 us
  waiting for transfers between devices  353 us (69%)
  blocking collectives  74.8 us (15%)
  matrix products  57.5 us (11%)
  between operations  14.2 us (3%)
  starting transfers between devices  8.28 us (2%)
    reduce_scatter x1, waiting for transfers between devices, local(): lax.psum_scatter(partial_grad, 'col', scatter_dimension=0, tiled=True)  88 us
    reduce_scatter x1, waiting for transfers between devices, local(): lax.psum_scatter(new_rows, 'row', scatter_dimension=0, tiled=True)  76.9 us
    all_gather x1, waiting for transfers between devices, local(): lax.all_gather(grid_grad, 'row', axis=0, tiled=True)  47.1 us
    all_gather x1, waiting for transfers between devices, local(): gate_piece = lax.all_gather(gate_block, 'col', axis=0, tiled=True)  46 us
    all_gather x1, waiting for transfers between devices, local(): hidden_piece = lax.all_gather(hidden_block, 'col', axis=0, tiled=True)  43.7 us
    psum x1, blocking collectives, local(): lax.psum(jnp.sum(lax.all_gather(gain_terms, 'col'), axis=0), 'row')  42.2 us
    all_gather x1, waiting for transfers between devices, local(): up_piece = lax.all_gather(up_block, 'col', axis=0, tiled=True)  40.7 us
    all_gather x1, blocking collectives, local(): lax.all_gather(gain_terms, 'col')  19.9 us
  transfers between devices with their start and end apart: 9, of which 8 were waited for; matrix products, arithmetic and copies ran while one was open for 4% of the time, Pallas kernels for 0%

profile of v1, /device:TPU:0, one launch (start us, length us, event | category | flops | bytes accessed | tf_op | source)
XLA Modules:
  0.0 513.6 jit_solution(8120245277999064050)
XLA Ops:
  7.2 0.0 all-gather.7.cloned.1.call-start
  7.2 12.6 %all_to_all.57 = bf16[8,16,512]{2,0,1:T(8,128)(2,1)} all-to-all(bf16[8,16,512]{2,0,1:T(8,128)(2,1)} %bitcast.28), channel_id=1, replica_groups=mesh['row'=8,'col'=16] {'col'}, dimensions={1} | all-to-all | bytes 262144 | tf_op jit(solution)/shard_map/all_to_all | solution.py:29
  19.9 0.0 all-gather.7.cloned.1.call-update
  19.9 0.0 reduce-scatter.3.cloned.1.call-start
  19.9 47.1 %all-gather.7.cloned.1.call-done = bf16[1024,512]{1,0:T(8,128)(2,1)} async-done(((bf16[128,512]{1,0:T(8,128)(2,1)}), bf16[1024,512]{1,0:T(8,128)(2,1)}) %all-gather.7.cloned.1.call-update) | async-done | bytes 1048592 | tf_op jit(solution)/shard_map/all_gather | solution.py:33
  67.1 11.6 %fusion.20 = f32[1024,3584]{1,0:T(8,128)} fusion(bf16[1024,512]{1,0:T(8,128)(2,1)} %all-gather.7.cloned.1.call-done, bf16[3584,512]{1,0:T(8,128)(2,1)} %param.15), kind=kOutput, calls=%fused_computation.34 | convolution fusion | flops 3758096384 | bytes 19398656 | tf_op jit(solution)/shard_map/td,fd->tf/dot_general | solution.py:35
  78.6 0.0 reduce-scatter.3.cloned.1.call-update
  78.7 0.0 all-gather.9.cloned.1.call-start
  78.7 88.0 %reduce-scatter.3.cloned.1.call-done = f32[64,3584]{1,0:T(8,128)} async-done(((f32[1024,3584]{1,0:T(8,128)}), f32[64,3584]{1,0:T(8,128)}) %reduce-scatter.3.cloned.1.call-update) | async-done | bytes 917520 | tf_op jit(solution)/shard_map/reduce_scatter | solution.py:38
  166.7 0.0 copy-done.3
  166.7 0.0 copy-done.4
  166.7 2.7 multiply_convert_fusion
  169.3 0.0 all-gather.9.cloned.1.call-update
  169.4 0.0 all-gather.11.cloned.1.call-start
  169.4 0.5 all-gather.11.cloned.1.call-update
  169.9 0.0 reduce-scatter.5.cloned.1.call-start
  170.0 46.0 %all-gather.9.cloned.1.call-done = bf16[1024,3584]{1,0:T(8,128)(2,1)} async-done(((bf16[64,3584]{1,0:T(8,128)(2,1)}), bf16[1024,3584]{1,0:T(8,128)(2,1)}) %all-gather.9.cloned.1.call-update) | async-done | bytes 7340048 | tf_op jit(solution)/shard_map/all_gather | solution.py:40
  216.0 9.4 %fusion.21 = f32[1024,512]{1,0:T(8,128)} fusion(bf16[1024,3584]{1,0:T(8,128)(2,1)} %all-gather.9.cloned.1.call-done, bf16[512,3584]{1,0:T(8,128)(2,1)} %param.13), kind=kOutput, calls=%fused_computation.35 | convolution fusion | flops 3758096384 | bytes 13107200 | tf_op jit(solution)/shard_map/tf,df->td/dot_general | solution.py:43
  225.5 40.7 %all-gather.11.cloned.1.call-done = bf16[1024,3584]{1,0:T(8,128)(2,1)} async-done(((bf16[64,3584]{1,0:T(8,128)(2,1)}), bf16[1024,3584]{1,0:T(8,128)(2,1)}) %all-gather.11.cloned.1.call-update) | async-done | bytes 7340048 | tf_op jit(solution)/shard_map/all_gather | solution.py:41
  266.2 10.1 %convolution_add_fusion = f32[1024,512]{1,0:T(8,128)} fusion(f32[1024,512]{1,0:T(8,128)} %fusion.21, bf16[1024,3584]{1,0:T(8,128)(2,1)} %all-gather.11.cloned.1.call-done, bf16[512,3584]{1,0:T(8,128)(2,1)} %param.14), kind=kOutput, calls=%fused_computation.3 | convolution fusion | flops 3758620672 | bytes 15204352 | tf_op jit(solution)/shard_map/tf,df->td/dot_general | solution.py:44
  276.3 0.0 reduce-scatter.5.cloned.1.call-update
  276.3 0.0 all-gather.15.cloned.1.call-start
  276.4 0.5 all-gather.15.cloned.1.call-update
  276.9 0.0 copy-done
  276.9 0.2 fusion.19
  277.1 76.9 %reduce-scatter.5.cloned.1.call-done = f32[128,512]{1,0:T(8,128)} async-done(((f32[1024,512]{1,0:T(8,128)}), f32[128,512]{1,0:T(8,128)}) %reduce-scatter.5.cloned.1.call-update) | async-done | bytes 262160 | tf_op jit(solution)/shard_map/reduce_scatter | solution.py:50
  354.0 4.5 all-to-all-start.1
  358.4 0.0 copy-start.5
  358.4 0.0 copy-start.2
  358.5 43.7 %all-gather.15.cloned.1.call-done = bf16[1024,3584]{1,0:T(8,128)(2,1)} async-done(((bf16[64,3584]{1,0:T(8,128)(2,1)}), bf16[1024,3584]{1,0:T(8,128)(2,1)}) %all-gather.15.cloned.1.call-update) | async-done | bytes 7340048 | tf_op jit(solution)/shard_map/all_gather | solution.py:42
  402.2 0.0 copy-done.6
  402.2 8.6 %convolution_convert_fusion = bf16[3584,512]{1,0:T(8,128)(2,1)} fusion(bf16[1024,3584]{1,0:T(8,128)(2,1)} %all-gather.15.cloned.1.call-done, bf16[1024,512]{1,0:T(8,128)(2,1)S(1)} %copy-done.6), kind=kOutput, calls=%fused_computation | convolution fusion | flops 3759931392 | bytes 12058624 | tf_op jit(solution)/shard_map/tf,td->fd/dot_general | solution.py:49
  410.8 0.0 all-to-all-done.1
  410.8 0.0 copy-done.5
  410.8 0.9 fusion.17
  411.7 19.9 %all-gather = f32[131072]{0:T(1024)S(1)} all-gather(f32[8192]{0:T(1024)S(1)} %get-tuple-element.5), channel_id=2, replica_groups=mesh['row'=8,'col'=16] {'col'}, dimensions={0}, use_global_device_ids=true | all-gather | bytes 557056 | tf_op jit(solution)/shard_map/all_gather | solution.py:53
  431.6 0.1 reshape.32
  431.8 3.5 all-to-all-start.2
  435.3 0.0 all-gather.13.cloned.1.call-start
  435.3 0.1 reduce_sum.39
  435.4 6.3 %all-to-all-done.2 = bf16[8,16,512]{2,0,1:T(8,128)(2,1)S(1)} async-done(((bf16[8,16,512]{2,0,1:T(8,128)(2,1)}), bf16[8,16,512]{2,0,1:T(8,128)(2,1)S(1)}, u32[]{:S(2)}, u32[]{:S(2)}) %all-to-all-start.2) | async-done | bytes 131104 | tf_op jit(solution)/shard_map/all_to_all | solution.py:28
  441.7 0.7 copy-done.1
  442.4 0.0 all-gather.13.cloned.1.call-update
  442.4 42.2 %psum.7 = f32[8192]{0:T(1024)} all-reduce(f32[8192]{0:T(1024)S(1)} %reduce_sum.39), channel_id=1, replica_groups=mesh['row'=8,'col'=16] {'row'}, use_global_device_ids=true, to_apply=%region_6.0 | all-reduce | flops 8192 | bytes 65536 | tf_op jit(solution)/shard_map/psum | solution.py:53
  484.7 0.8 fusion.16
  485.4 3.4 all-gather.13.cloned.1.call-done
  488.9 9.3 %convolution_convert_fusion.2 = bf16[512,3584]{1,0:T(8,128)(2,1)} fusion(bf16[1024,512]{1,0:T(8,128)(2,1)} %all-gather.13.cloned.1.call-done, bf16[1024,3584]{1,0:T(8,128)(2,1)} %all-gather.9.cloned.1.call-done), kind=kOutput, calls=%fused_computation.2 | convolution fusion | flops 3759931392 | bytes 12058624 | tf_op jit(solution)/shard_map/td,tf->df/dot_general | solution.py:47
  498.2 8.5 %convolution_convert_fusion.1 = bf16[512,3584]{1,0:T(8,128)(2,1)} fusion(bf16[1024,512]{1,0:T(8,128)(2,1)S(1)} %copy-done.7, bf16[1024,3584]{1,0:T(8,128)(2,1)} %all-gather.11.cloned.1.call-done), kind=kOutput, calls=%fused_computation.1 | convolution fusion | flops 3759931392 | bytes 12058624 | tf_op jit(solution)/shard_map/td,tf->df/dot_general | solution.py:48
  (10 shorter events, 0.0 us)
Async XLA Ops:
  7.2 59.9 %all-gather.7.cloned.1.call-start = ((), (), s32[]{:S(2)}) async-start(), calls=%async_computation.5 | async-start | bytes 1179648 | tf_op jit(solution)/shard_map/all_gather | solution.py:33
  19.9 146.8 %reduce-scatter.3.cloned.1.call-start = ((), (), s32[]{:S(2)}) async-start(), calls=%async_computation.6 | async-start | bytes 15597568 | tf_op jit(solution)/shard_map/reduce_scatter | solution.py:38
  78.6 88.0 %copy-start.3 = (bf16[64,3584]{1,0:T(8,128)(2,1)S(1)}, bf16[64,3584]{1,0:T(8,128)(2,1)}, u32[]{:S(2)}) copy-start(bf16[64,3584]{1,0:T(8,128)(2,1)} %param.11) | copy-start | bytes 1376260
  78.6 88.0 %copy-start.4 = (bf16[64,3584]{1,0:T(8,128)(2,1)S(1)}, bf16[64,3584]{1,0:T(8,128)(2,1)}, u32[]{:S(2)}) copy-start(bf16[64,3584]{1,0:T(8,128)(2,1)} %param.12) | copy-start | bytes 1376260
  78.7 137.4 %all-gather.9.cloned.1.call-start = ((), (), s32[]{:S(2)}) async-start(), calls=%async_computation.7 | async-start | bytes 7798784 | tf_op jit(solution)/shard_map/all_gather | solution.py:40
  169.4 96.8 %all-gather.11.cloned.1.call-start = ((), (), s32[]{:S(2)}) async-start(), calls=%async_computation.8 | async-start | bytes 7798784 | tf_op jit(solution)/shard_map/all_gather | solution.py:41
  169.9 184.0 %reduce-scatter.5.cloned.1.call-start = ((), (), s32[]{:S(2)}) async-start(), calls=%async_computation.9 | async-start | bytes 2359296 | tf_op jit(solution)/shard_map/reduce_scatter | solution.py:50
  225.4 51.4 %copy-start = (bf16[8,8192]{1,0:T(8,128)(2,1)S(1)}, bf16[8,8192]{1,0:T(8,128)(2,1)}, u32[]{:S(2)}) copy-start(bf16[8,8192]{1,0:T(8,128)(2,1)} %param.8) | copy-start | bytes 393220
  225.4 176.8 %copy-start.6 = (bf16[1024,512]{1,0:T(8,128)(2,1)S(1)}, bf16[1024,512]{1,0:T(8,128)(2,1)}, u32[]{:S(2)}) copy-start(bf16[1024,512]{1,0:T(8,128)(2,1)} %all-gather.7.cloned.1.call-done) | copy-start | bytes 3145732
  276.3 125.9 %all-gather.15.cloned.1.call-start = ((), (), s32[]{:S(2)}) async-start(), calls=%async_computation.11 | async-start | bytes 7798784 | tf_op jit(solution)/shard_map/all_gather | solution.py:42
  354.0 56.8 %all-to-all-start.1 = ((f32[16,8,512]{2,1,0:T(8,128)}), f32[16,8,512]{2,1,0:T(8,128)S(1)}, u32[]{:S(2)}, u32[]{:S(2)}) async-start(f32[16,8,512]{2,1,0:T(8,128)} %bitcast.29), calls=%async_computation.3 | async-start | bytes 524288 | tf_op jit(solution)/shard_map/all_to_all | solution.py:51
  358.4 52.4 %copy-start.5 = (f32[8192]{0:T(1024)S(1)}, f32[8192]{0:T(1024)}, u32[]{:S(2)}) copy-start(f32[8192]{0:T(1024)} %param.9) | copy-start | bytes 98308
  358.4 126.2 %copy-start.2 = (bf16[8,8192]{1,0:T(8,128)(2,1)S(1)}, bf16[8,8192]{1,0:T(8,128)(2,1)}, u32[]{:S(2)}) copy-start(bf16[8,8192]{1,0:T(8,128)(2,1)} %param.10) | copy-start | bytes 393220
  431.8 10.0 %all-to-all-start.2 = ((bf16[8,16,512]{2,0,1:T(8,128)(2,1)}), bf16[8,16,512]{2,0,1:T(8,128)(2,1)S(1)}, u32[]{:S(2)}, u32[]{:S(2)}) async-start(bf16[8,16,512]{2,0,1:T(8,128)(2,1)} %bitcast.7), calls=%async_computation.4 | async-start | bytes 262144 | tf_op jit(solution)/shard_map/all_to_all | solution.py:28
  435.3 53.6 %all-gather.13.cloned.1.call-start = ((), (), s32[]{:S(2)}) async-start(), calls=%async_computation.10 | async-start | bytes 1179648 | tf_op jit(solution)/shard_map/all_gather | solution.py:32
  441.7 0.7 copy-start.1
  488.9 9.3 %copy-start.7 = (bf16[1024,512]{1,0:T(8,128)(2,1)S(1)}, bf16[1024,512]{1,0:T(8,128)(2,1)}, u32[]{:S(2)}) copy-start(bf16[1024,512]{1,0:T(8,128)(2,1)} %all-gather.13.cloned.1.call-done) | copy-start | bytes 3145732
Sparse Core Ops, SparseCore 0:
  20.0 47.0 all-gather.6
  78.8 87.8 reduce-scatter.2
  169.5 46.5 all-gather.8
  218.2 47.9 all-gather.10
  276.4 77.4 reduce-scatter.4
  356.1 46.0 all-gather.14
  442.5 46.2 all-gather.12
